TPU v7x, 32 devices: a whole 2x2x4 slice. The times are simulated.
32 devices in a mesh: grp: 2 (over y), tm: 4 (over z), height: 4 (over x, core).
Axes of the slice: x: 2, y: 2, z: 4, core: 2. Of those that a mesh axis runs over, the one named last changes fastest.
Arguments:
- latents: bfloat16 [8, 8, 160, 384], P(('grp', 'tm'), 'height'), parts along dimension 0, may hold values from -6 to 6
- gain: float32 [384], replicated, may hold values from 0.1 to 1.9
- bias: float32 [384], replicated, may hold values from -3 to 3
- weight: bfloat16 [10368, 384], replicated, may hold values from -0.0625 to 0.0625
- cotangent: bfloat16 [8, 8, 160, 384], P(('grp', 'tm'), 'height'), parts along dimension 0, may hold values from -6 to 6
Outputs:
- output: bfloat16 [8, 8, 160, 384], P(('grp', 'tm'), 'height'), parts along dimension 0
- latent_grad: bfloat16 [8, 8, 160, 384], P(('grp', 'tm'), 'height'), parts along dimension 0
- weight_grad: float32 [20736, 384], P(('grp', 'tm'), 'height'), parts along dimension 0
There are 2 independent parts, one for each index of `grp`. A program takes and returns all parts, laid end to end along the dimension named above; an argument that names none is the same for every part. Nothing has to cross between parts.
All inputs are finite; a program needn't handle non-finite values.
Results may differ from a plain program's by a relative error of at most 0.0029.
Values may be sent and summed in bfloat16 or wider, within the bound.
No kernel may reach another device: no remote copies, remote signals or barrier semaphores. Data moves between devices by JAX's collectives and lax.ppermute only.
A program may use at most 128 MiB of HBM per device.

v0:
```python
import math
import jax
import jax.numpy as jnp
from jax import lax
from jax.sharding import PartitionSpec as P


def shifted_2(value, axis, by):
    devices = lax.axis_size(axis)
    pairs = [(i, i + by) for i in range(devices) if 0 <= i + by < devices]
    return lax.ppermute(value, axis, pairs)


def padded(cells, sides, width):
    for axis, dim in sides:
        count = lax.axis_size(axis)
        ends = count - 1
        head = lax.slice_in_dim(cells, 0, width, axis=dim)
        tail = lax.slice_in_dim(cells, cells.shape[dim] - width, cells.shape[dim], axis=dim)
        cells = jnp.concatenate(
            [
                lax.ppermute(tail, axis, [(i, (i + 1) % count) for i in range(ends)]),
                cells,
                lax.ppermute(head, axis, [((i + 1) % count, i) for i in range(ends)]),
            ],
            axis=dim,
        )
    return cells


def forward_arrange(cube):
    depth, rows_t, cols_t, inputs, outputs = cube.shape
    return cube.transpose(0, 1, 3, 2, 4).reshape(9, inputs, 3 * outputs)


def backward_arrange(cube):
    depth, rows_t, cols_t, inputs, outputs = cube.shape
    return cube.transpose(0, 1, 4, 2, 3).reshape(9, outputs, 3 * inputs)


def forward_conv(window, cube, row_total, col_total):
    window = window[:, :, : col_total + 2]
    result = lax.conv_general_dilated(
        window[None],
        cube,
        (1, 1, 1),
        "VALID",
        dimension_numbers=("NDHWC", "DHWIO", "NDHWC"),
        preferred_element_type=jnp.float32,
    )
    return result[0, 0]


def backward_conv(window, cube, row_total, col_total):
    window = window[:, :, : col_total + 2]
    result = lax.conv_general_dilated(
        window[None],
        jnp.flip(cube, (0, 1, 2)),
        (1, 1, 1),
        "VALID",
        dimension_numbers=("NDHWC", "DHWOI", "NDHWC"),
        preferred_element_type=jnp.float32,
    )
    return result[0, 0]


def pair_count(tap_rows, share_rows, pair_rows, parts):
    most = 1
    for index in range(parts):
        first = index * share_rows
        last = first + share_rows - 1
        most = max(most, last // pair_rows - first // pair_rows + 1)
    return most


def depth_span(share_rows, tap_rows, channels):
    plane_rows = 9 * channels
    most = 1
    for index in range(tap_rows // share_rows):
        first = index * share_rows
        last = first + share_rows - 1
        most = max(most, last // plane_rows - first // plane_rows + 1)
    return most


def block_weight_grad(framed, cot_all, frame_index, share_rows, channels):
    frame_total, row_total, col_total, slots = cot_all.shape
    plane_rows = 9 * channels
    tap_rows = 27 * channels
    span = depth_span(share_rows, tap_rows, channels)
    first_row = frame_index * share_rows
    first_depth = jnp.minimum(first_row // plane_rows, 3 - span)
    frames = lax.dynamic_slice_in_dim(framed, first_depth, frame_total + span - 1, 0)
    frames = frames[:, :, : col_total + 2]
    terms = lax.conv_general_dilated(
        frames[..., None],
        cot_all[:, :, :, None, :],
        (1, 1, 1),
        "VALID",
        dimension_numbers=("DHWNC", "DHWIO", "DHWNC"),
        preferred_element_type=jnp.float32,
    ).reshape(span * plane_rows, slots)
    return lax.dynamic_slice_in_dim(terms, first_row - first_depth * plane_rows, share_rows, 0)


def gather_rows(own, height_count):
    frame_total, row_count, col_count, channels = own.shape
    height_index = lax.axis_index("height")
    core = height_index % 2
    chip = height_index // 2
    chips = height_count // 2
    first = core == 0
    sibling = [(i, i ^ 1) for i in range(height_count)]
    mine = [own] + [
        lax.ppermute(
            own, "height", [(i, (i + 2 * step) % height_count) for i in range(height_count)]
        )
        for step in range(1, chips)
    ]
    stacked = jnp.concatenate(mine, axis=1)
    twins = lax.ppermute(stacked, "height", sibling)
    block = 2 * row_count
    relative = []
    for step in reversed(range(chips)):
        ours = stacked[:, step * row_count : (step + 1) * row_count]
        theirs = twins[:, step * row_count : (step + 1) * row_count]
        relative.append(
            jnp.where(
                first,
                jnp.concatenate([ours, theirs], axis=1),
                jnp.concatenate([theirs, ours], axis=1),
            )
        )
    relative = jnp.concatenate(relative, axis=1)
    return jnp.concatenate(
        [
            lax.dynamic_slice_in_dim(relative, (place - chip - 1) % chips * block, block, 1)
            for place in range(chips)
        ],
        axis=1,
    )


def local(latents, gain, bias, weight, cotangent):
    frame_count, row_count, col_count, channels = latents.shape
    latent_wide = latents.astype(jnp.float32)
    root_mean = jnp.sqrt(jnp.mean(latent_wide * latent_wide, axis=-1, keepdims=True) + 1e-06)
    normed = latent_wide / root_mean * gain
    hidden = jax.nn.silu(normed).astype(jnp.bfloat16)
    height_count = lax.axis_size("height")
    frame_devices = lax.axis_size("tm")
    frame_index = lax.axis_index("tm")
    row_index = lax.axis_index("height")
    total_rows = row_count * height_count
    total_frames = frame_count * frame_devices
    tap_rows = 27 * channels
    share_rows = tap_rows // frame_devices
    padded_cols = col_count + 2
    right_pad = padded_cols - col_count - 1
    inverse_root = 1.0 / math.sqrt(total_frames * total_rows * col_count)
    weight_cube = weight.reshape(3, 3, 3, channels, channels)
    both_frames = lax.all_gather(
        jnp.concatenate([hidden, cotangent], axis=-1), "tm", axis=0, tiled=True
    )
    hidden_all = gather_rows(both_frames[..., :channels], height_count)
    framed = jnp.pad(hidden_all, ((2, 0), (1, 1), (1, right_pad), (0, 0)))
    cot_frames = both_frames[..., channels:]
    cot_all = lax.all_to_all(cot_frames, "height", split_axis=3, concat_axis=1, tiled=True)
    window = lax.dynamic_slice(
        framed,
        (frame_index * frame_count, row_index * row_count, 0, 0),
        (frame_count + 2, row_count + 2, padded_cols, channels),
    )
    conv_out = forward_conv(window, weight_cube, row_count, col_count).reshape(
        frame_count, row_count, col_count, channels
    )
    output = (latent_wide + conv_out + bias).astype(jnp.bfloat16)
    weight_grad = (
        block_weight_grad(framed, cot_all, frame_index, share_rows, channels) * inverse_root
    )
    cot_future = lax.dynamic_slice_in_dim(
        jnp.pad(cot_frames, ((0, 2), (0, 0), (0, 0), (0, 0))), frame_index * frame_count, 3, 0
    )
    cotangent_edged = padded(cot_future, (("height", 1),), 1)
    future_block = jnp.pad(cotangent_edged, ((0, 0), (0, 0), (1, right_pad), (0, 0)))
    hidden_grad = backward_conv(future_block, weight_cube, row_count, col_count).reshape(
        frame_count, row_count, col_count, channels
    )
    sigmoid_pre = jax.nn.sigmoid(normed)
    normed_grad = hidden_grad * sigmoid_pre * (1.0 + normed * (1.0 - sigmoid_pre))
    scaled_grad = normed_grad * gain
    unit_latent = latent_wide / root_mean
    inner = jnp.mean(scaled_grad * unit_latent, axis=-1, keepdims=True)
    latent_grad = (
        cotangent.astype(jnp.float32) + (scaled_grad - unit_latent * inner) / root_mean
    ).astype(jnp.bfloat16)
    return (output, latent_grad, weight_grad)


def solution(mesh):
    placed = (
        P(("grp", "tm"), "height", None, None),
        P(),
        P(),
        P(),
        P(("grp", "tm"), "height", None, None),
    )
    return jax.shard_map(
        local,
        mesh=mesh,
        in_specs=placed,
        out_specs=(
            P(("grp", "tm"), "height", None, None),
            P(("grp", "tm"), "height", None, None),
            P(("grp", "tm"), "height"),
        ),
        check_vma=False,
    )
```

profile of v0, /device:TPU:0, one launch (start us, length us, event | category | flops | bytes accessed | tf_op | source)
XLA Modules:
  0.0 224.5 jit_solution(6320341675211582955)
XLA Ops:
  8.3 1.2 multiply_convert_fusion
  9.5 1.8 pad_maximum_fusion.3
  11.3 46.4 %all-gather.2.cloned.1.call-done = bf16[4,2,160,768]{3,2,1,0:T(8,128)(2,1)} async-done(((bf16[1,2,160,768]{3,2,1,0:T(8,128)(2,1)}), bf16[4,2,160,768]{3,2,1,0:T(8,128)(2,1)}) %all-gather.2.cloned.1.call-update) | async-done | bytes 1966096 | tf_op jit(solution)/shard_map/all_gather | solution.py:162
  57.7 1.7 fusion.61
  59.4 1.5 collective-permute-start
  62.0 1.3 collective-permute-start.3
  63.3 3.8 %collective-permute-start.2 = (bf16[3,1,160,384]{3,2,1,0:T(8,128)(2,1)}, bf16[3,1,160,384]{3,2,1,0:T(8,128)(2,1)}, u32[]{:S(2)}, u32[]{:S(2)}) collective-permute-start(bf16[3,1,160,384]{3,2,1,0:T(8,128)(2,1)} %get-tuple-element.21), channel_id=1, source_target_pairs={{0,1},{1,2},{2,3},{4,5},{5,6},{6,7},{8,9},{9,10},{10,11},{12,13},{... | collective-permute-start | bytes 1105928 | tf_op jit(solution)/shard_map/ppermute | solution.py:22
  67.1 16.1 %collective-permute-done = bf16[4,2,160,384]{3,2,1,0:T(8,128)(2,1)S(1)} collective-permute-done((bf16[4,2,160,384]{3,2,1,0:T(8,128)(2,1)S(1)}, bf16[4,2,160,384]{3,2,1,0:T(8,128)(2,1)S(1)}, u32[]{:S(2)}, u32[]{:S(2)}) %collective-permute-start) | collective-permute-done | bytes 983072 | tf_op jit(solution)/shard_map/ppermute | solution.py:115
  83.1 1.6 pad_maximum_fusion.1
  84.8 2.5 %copy.92 = bf16[4,2,160,384]{2,0,1,3:T(4,128)(2,1)} copy(bf16[4,2,160,384]{3,2,1,0:T(8,128)(2,1)S(1)} %get-tuple-element.17) | data formatting | bytes 1966080 | tf_op jit(solution)/shard_map/slice | solution.py:167
  87.3 3.9 %all-to-all-start = ((bf16[4,2,160,384]{2,0,1,3:T(4,128)(2,1)}), bf16[4,2,160,384]{2,0,1,3:T(4,128)(2,1)S(1)}, u32[]{:S(2)}, u32[]{:S(2)}) async-start(bf16[4,2,160,384]{2,0,1,3:T(4,128)(2,1)} %copy.92), calls=%async_computation | async-start | bytes 3145728 | tf_op jit(solution)/shard_map/all_to_all | solution.py:168
  91.3 1.6 fusion.40
  94.3 7.1 %fusion.41 = f32[1,2,8,21,384]{4,2,3,1,0:T(8,128)S(1)} fusion(bf16[3,3,3,384,384]{4,3,2,1,0:T(8,128)(2,1)} %bitcast.52, bf16[3,4,1,7,2,384]{5,3,4,1,0,2:T(8,128)(2,1)S(1)} %slice.34, bf16[3,4,1,8,21,384]{5,3,4,1,0,2:T(8,128)(2,1)S(1)} %copy.89, pred[8,21]{0,1:T(8,128)(4,1)S(1)} %copy-done.7), kind=kOutput, calls=%fused_computation.59 | convolution fusion | flops 2680657920 | bytes 10156200 | tf_op jit(solution)/shard_map/conv_general_dilated | solution.py:56
  102.7 9.1 %all-to-all-done = bf16[4,2,160,384]{2,0,1,3:T(4,128)(2,1)S(1)} async-done(((bf16[4,2,160,384]{2,0,1,3:T(4,128)(2,1)}), bf16[4,2,160,384]{2,0,1,3:T(4,128)(2,1)S(1)}, u32[]{:S(2)}, u32[]{:S(2)}) %all-to-all-start) | async-done | bytes 983072 | tf_op jit(solution)/shard_map/all_to_all | solution.py:168
  111.7 2.5 %copy.94 = bf16[4,4,2,160,96]{4,3,2,1,0:T(8,128)(2,1)} copy(bf16[4,4,2,160,96]{3,0,2,4,1:T(4,128)(2,1)S(1)} %bitcast.46) | data formatting | bytes 1966080 | tf_op jit(solution)/shard_map/all_to_all | solution.py:168
  114.3 1.7 fusion.62
  117.5 1.6 fusion.20
  119.2 5.8 %fusion.10 = bf16[6,10,162,384]{3,2,1,0:T(8,128)(2,1)S(1)} fusion(bf16[4,4,160,384]{3,2,1,0:T(8,128)(2,1)S(1)} %get-tuple-element.16, bf16[4,4,160,384]{3,2,1,0:T(8,128)(2,1)S(1)} %get-tuple-element.15), kind=kLoop, calls=%fused_computation.15 | loop fusion | flops 70917120 | bytes 11397120 | tf_op jit(solution)/shard_map/concatenate | solution.py:135
  127.1 3.8 %fusion.44 = f32[1,2,8,21,384]{4,2,3,1,0:T(8,128)S(1)} fusion(bf16[3,3,3,384,384]{4,3,2,1,0:T(8,128)(2,1)S(1)} %bitcast.55, bf16[3,4,1,7,2,384]{5,3,4,1,0,2:T(8,128)(2,1)S(1)} %slice.31, bf16[3,4,1,8,21,384]{5,3,4,1,0,2:T(8,128)(2,1)S(1)} %copy.84, pred[8,21]{0,1:T(8,128)(4,1)S(1)} %copy-done.7), kind=kOutput, calls=%fused_computation.60 | convolution fusion | flops 2680657920 | bytes 10156200 | tf_op jit(solution)/shard_map/conv_general_dilated | solution.py:43
  133.5 74.5 %fusion.6 = f32[2,3,3,384,96]{3,4,2,1,0:T(8,128)S(1)} fusion(bf16[5,10,162,384,1]{3,2,1,0,4:T(8,128)(2,1)S(1)} %dynamic-slice_bitcast_fusion, bf16[4,8,160,1,96]{4,2,1,0,3:T(8,128)(2,1)S(1)} %bitcast.51), kind=kOutput, calls=%fused_computation.11 | convolution fusion | flops 6794772480 | bytes 9858048 | tf_op jit(solution)/shard_map/conv_general_dilated | solution.py:95
  207.9 1.8 copy.97
  209.8 2.8 %reshape.42 = f32[6912,96]{0,1:T(8,128)} reshape(f32[2,3,3,384,96]{3,2,1,0,4:T(4,128)S(1)} %copy.97) | data formatting | bytes 5308416 | tf_op jit(solution)/shard_map/reshape | solution.py:102
  212.6 2.5 %dynamic-slice_multiply_fusion = f32[2592,96]{0,1:T(8,128)} fusion(f32[6912,96]{0,1:T(8,128)} %reshape.42, s32[]{:T(128)S(6)} %select_n.66), kind=kLoop, calls=%fused_computation.61 | loop fusion | flops 248832 | bytes 1990660 | tf_op jit(solution)/shard_map/mul | solution.py:179
  215.1 2.6 %add_convert_fusion = (bf16[1,2,160,384]{3,2,1,0:T(8,128)(2,1)}, bf16[1,2,160,384]{3,2,1,0:T(8,128)(2,1)}) fusion(bf16[1,2,160,384]{3,2,1,0:T(8,128)(2,1)} %param.9, f32[2,160]{1,0:T(2,128)S(1)} %broadcast_multiply_fusion, f32[2,160]{1,0:T(2,128)S(1)} %add_sqrt_fusion, f32[384]{0:T(512)S(1)} %copy-done.5, f32[1,2,1,160,384]{4,1,3,2,0:T(2,128)} %copy-done, ...), kind=kLoop, calls=%fused_computation.76 | loop fusion | flops 2580480 | bytes 1971712 | tf_op jit(solution)/shard_map/convert_element_type | solution.py:196
  (49 shorter events, 11.0 us)
Async XLA Ops:
  7.2 50.6 %all-gather.2.cloned.1.call-start = ((), (), s32[]{:S(2)}) async-start(), calls=%async_computation.1 | async-start | bytes 2457600 | tf_op jit(solution)/shard_map/all_gather | solution.py:162
  59.4 23.7 %collective-permute-start = (bf16[4,2,160,384]{3,2,1,0:T(8,128)(2,1)S(1)}, bf16[4,2,160,384]{3,2,1,0:T(8,128)(2,1)S(1)}, u32[]{:S(2)}, u32[]{:S(2)}) collective-permute-start(bf16[4,2,160,384]{3,2,1,0:T(8,128)(2,1)S(1)} %get-tuple-element.18), channel_id=1, source_target_pairs={{0,2},{1,3},{2,0},{3,1},{4,6},{5,7},{6,4},{7,5},{8,10},{9,11},{10,... | collective-permute-start | bytes 2949128 | tf_op jit(solution)/shard_map/ppermute | solution.py:115
  62.0 29.3 %collective-permute-start.3 = (bf16[3,1,160,384]{3,2,1,0:T(8,128)(2,1)}, bf16[3,1,160,384]{3,2,1,0:T(8,128)(2,1)}, u32[]{:S(2)}, u32[]{:S(2)}) collective-permute-start(bf16[3,1,160,384]{3,2,1,0:T(8,128)(2,1)} %get-tuple-element.22), channel_id=1, source_target_pairs={{1,0},{2,1},{3,2},{5,4},{6,5},{7,6},{9,8},{10,9},{11,10},{13,12},{... | collective-permute-start | bytes 1105928 | tf_op jit(solution)/shard_map/ppermute | solution.py:24
  63.3 28.0 %collective-permute-start.2 = (bf16[3,1,160,384]{3,2,1,0:T(8,128)(2,1)}, bf16[3,1,160,384]{3,2,1,0:T(8,128)(2,1)}, u32[]{:S(2)}, u32[]{:S(2)}) collective-permute-start(bf16[3,1,160,384]{3,2,1,0:T(8,128)(2,1)} %get-tuple-element.21), channel_id=1, source_target_pairs={{0,1},{1,2},{2,3},{4,5},{5,6},{6,7},{8,9},{9,10},{10,11},{12,13},{... | collective-permute-start | bytes 1105928 | tf_op jit(solution)/shard_map/ppermute | solution.py:22
  83.1 4.2 %copy-start.2 = (bf16[4,2,160,384]{3,2,1,0:T(8,128)(2,1)}, bf16[4,2,160,384]{3,2,1,0:T(8,128)(2,1)S(1)}, u32[]{:S(2)}) copy-start(bf16[4,2,160,384]{3,2,1,0:T(8,128)(2,1)S(1)} %collective-permute-done) | copy-start | bytes 2949124
  84.7 29.5 %collective-permute-start.1 = (bf16[4,4,160,384]{3,2,1,0:T(8,128)(2,1)}, bf16[4,4,160,384]{3,2,1,0:T(8,128)(2,1)}, u32[]{:S(2)}, u32[]{:S(2)}) collective-permute-start(bf16[4,4,160,384]{3,2,1,0:T(8,128)(2,1)} %pad_maximum_fusion.1), channel_id=1, source_target_pairs={{0,1},{1,0},{2,3},{3,2},{4,5},{5,4},{6,7},{7,6},{8,9},{9,8},{10,11... | collective-permute-start | bytes 5898248 | tf_op jit(solution)/shard_map/ppermute | solution.py:121
  87.3 24.4 %all-to-all-start = ((bf16[4,2,160,384]{2,0,1,3:T(4,128)(2,1)}), bf16[4,2,160,384]{2,0,1,3:T(4,128)(2,1)S(1)}, u32[]{:S(2)}, u32[]{:S(2)}) async-start(bf16[4,2,160,384]{2,0,1,3:T(4,128)(2,1)} %copy.92), calls=%async_computation | async-start | bytes 3145728 | tf_op jit(solution)/shard_map/all_to_all | solution.py:168
  93.4 0.9 copy-start.7
  94.3 7.6 %copy-start.1 = (bf16[1,2,160,384]{3,2,1,0:T(8,128)(2,1)S(1)}, bf16[1,2,160,384]{3,2,1,0:T(8,128)(2,1)}, u32[]{:S(2)}) copy-start(bf16[1,2,160,384]{3,2,1,0:T(8,128)(2,1)} %param.5) | copy-start | bytes 737284
  94.3 7.6 %copy-start.5 = (f32[384]{0:T(512)S(1)}, f32[384]{0:T(512)}, u32[]{:S(2)}) copy-start(f32[384]{0:T(512)} %param.6) | copy-start | bytes 4612
  101.9 0.8 copy-start
  116.0 1.2 copy-start.3
  119.2 7.5 %slice-start = ((s8[7962624]{0:T(1024)(128)(4,1)}), s8[4194304]{0:T(1024)(128)(4,1)S(1)}, s32[]{:S(2)}) async-start(s8[7962624]{0:T(1024)(128)(4,1)} %bitcast.53), calls=%async_computation.2 | async-start | bytes 8388608
  125.0 2.1 slice-start.1
  132.1 1.3 copy-start.4
  209.7 5.3 %copy-start.6 = (f32[384]{0:T(512)S(1)}, f32[384]{0:T(512)}, u32[]{:S(2)}) copy-start(f32[384]{0:T(512)} %param.7) | copy-start | bytes 4612
Sparse Core Ops, SparseCore 0:
  11.4 46.2 all-gather.1
where the time goes:
time: 225 us; the launch traced here: 224 us
  matrix products  85.4 us (38%)
  waiting for transfers between devices  71.6 us (32%)
  local copies, waits for them, and re-layouts  21.8 us (10%)
  other arithmetic  20.9 us (9%)
  between operations  14.3 us (6%)
  starting transfers between devices  10.5 us (5%)
    conv_general_dilated x1, matrix products, block_weight_grad(): lax.conv_general_dilated(frames[..., None], cot_all[:, :, :, None, :], (1...  74.5 us
    all_gather x1, waiting for transfers between devices, local(): lax.all_gather(jnp.concatenate([hidden, cotangent], axis=-1), 'tm', axis=...  46.4 us
    ppermute x1, waiting for transfers between devices, gather_rows(): lax.ppermute(own, 'height', [(i, (i + 2 * step) % height_count) for i in...  16.1 us
    all_to_all x1, waiting for transfers between devices, local(): lax.all_to_all(cot_frames, 'height', split_axis=3, concat_axis=1, tiled=T...  9.06 us
    conv_general_dilated x1, matrix products, backward_conv(): lax.conv_general_dilated(window[None], jnp.flip(cube, (0, 1, 2)), (1, 1,...  7.08 us
    concatenate x1, other arithmetic, gather_rows(): jnp.concatenate([lax.dynamic_slice_in_dim(relative, (place - chip - 1) %...  5.81 us
  transfers between devices with their start and end apart: 6, of which 3 were waited for; matrix products, arithmetic and copies ran while one was open for 8% of the time, Pallas kernels for 0%

commit v1 on v0

--- a/solution.py
+++ b/solution.py
@@ -3,6 +3,24 @@
 import jax.numpy as jnp
 from jax import lax
 from jax.sharding import PartitionSpec as P
+
+
+def ring_gather(shard, axis, dim):
+    ways, here, hop = (lax.axis_size(axis), lax.axis_index(axis), shard.shape[dim])
+    lengths = [n * ways if d == dim else n for d, n in enumerate(shard.shape)]
+    full = lax.dynamic_update_slice_in_dim(
+        jnp.zeros(lengths, shard.dtype), shard, here * hop, axis=dim
+    )
+    going_up = going_down = shard
+    for far in range(1, ways // 2 + 1):
+        going_up = lax.ppermute(going_up, axis, [(d, (d + 1) % ways) for d in range(ways)])
+        full = lax.dynamic_update_slice_in_dim(full, going_up, (here - far) % ways * hop, axis=dim)
+        if 2 * far < ways:
+            going_down = lax.ppermute(going_down, axis, [(d, (d - 1) % ways) for d in range(ways)])
+            full = lax.dynamic_update_slice_in_dim(
+                full, going_down, (here + far) % ways * hop, axis=dim
+            )
+    return full
 
 
 def shifted_2(value, axis, by):
@@ -159,9 +177,7 @@
     right_pad = padded_cols - col_count - 1
     inverse_root = 1.0 / math.sqrt(total_frames * total_rows * col_count)
     weight_cube = weight.reshape(3, 3, 3, channels, channels)
-    both_frames = lax.all_gather(
-        jnp.concatenate([hidden, cotangent], axis=-1), "tm", axis=0, tiled=True
-    )
+    both_frames = ring_gather(jnp.concatenate([hidden, cotangent], axis=-1), "tm", 0)
     hidden_all = gather_rows(both_frames[..., :channels], height_count)
     framed = jnp.pad(hidden_all, ((2, 0), (1, 1), (1, right_pad), (0, 0)))
     cot_frames = both_frames[..., channels:]

time: 225 us -> 207 us (0.920)
  waiting for transfers between devices: 71.6 us -> 55.2 us
  between operations: 14.3 us -> 0.97 us
  local copies, waits for them, and re-layouts: 21.8 us -> 29.9 us
  starting transfers between devices: 10.5 us -> 15.6 us
    all_gather x1 -> x0, waiting for transfers between devices: 46.4 us -> none  [local(): lax.all_gather(jnp.concatenate([hidden, cotangent], axis=-1), 'tm', axis=...]
    ppermute x0 -> x3, waiting for transfers between devices: none -> 30.7 us  [the longest x2 22.3 us: ring_gather(): lax.ppermute(going_up, axis, [(d, (d + 1) % ways) for d in range(ways)])]
    ppermute x0 -> x3, starting transfers between devices: none -> 5.07 us  [the longest x2 3.01 us: ring_gather(): lax.ppermute(going_up, axis, [(d, (d + 1) % ways) for d in range(ways)])]
    all_to_all x1 -> x2, local copies, waits for them, and re-layouts: 2.54 us -> 5.96 us  [local(): lax.all_to_all(cot_frames, 'height', split_axis=3, concat_axis=1, tiled=T...]
    dynamic_update_slice x0 -> x3, local copies, waits for them, and re-layouts: none -> 2.48 us  [the longest x2 1.67 us: ring_gather(): lax.dynamic_update_slice_in_dim(full, going_up, (here - far) % ways * hop...]
  transfers between devices with their start and end apart: 6 -> 8, of which waited for: 3 -> 5; matrix products, arithmetic and copies ran while one was open for 8% -> 12% of each run, Pallas kernels for 0% -> 0%
where the time goes in v1:
time: 207 us; the launch traced here: 206 us
  matrix products  85.7 us (41%)
  waiting for transfers between devices  55.2 us (27%)
  local copies, waits for them, and re-layouts  29.9 us (14%)
  other arithmetic  18.8 us (9%)
  starting transfers between devices  15.6 us (8%)
    conv_general_dilated x1, matrix products, block_weight_grad(): lax.conv_general_dilated(frames[..., None], cot_all[:, :, :, None, :], (1...  74.8 us
    ppermute x2, waiting for transfers between devices, ring_gather(): lax.ppermute(going_up, axis, [(d, (d + 1) % ways) for d in range(ways)])  22.3 us
    ppermute x1, waiting for transfers between devices, gather_rows(): lax.ppermute(own, 'height', [(i, (i + 2 * step) % height_count) for i in...  16.1 us
    all_to_all x1, waiting for transfers between devices, local(): lax.all_to_all(cot_frames, 'height', split_axis=3, concat_axis=1, tiled=T...  8.42 us
    ppermute x1, waiting for transfers between devices, ring_gather(): lax.ppermute(going_down, axis, [(d, (d - 1) % ways) for d in range(ways)])  8.4 us
    conv_general_dilated x1, matrix products, backward_conv(): lax.conv_general_dilated(window[None], jnp.flip(cube, (0, 1, 2)), (1, 1,...  7.03 us
    all_to_all x2, local copies, waits for them, and re-layouts, local(): lax.all_to_all(cot_frames, 'height', split_axis=3, concat_axis=1, tiled=T...  5.96 us
    concatenate x1, other arithmetic, gather_rows(): jnp.concatenate([lax.dynamic_slice_in_dim(relative, (place - chip - 1) %...  5.85 us
  transfers between devices with their start and end apart: 8, of which 5 were waited for; matrix products, arithmetic and copies ran while one was open for 12% of the time, Pallas kernels for 0%

profile of v1, /device:TPU:0, one launch (start us, length us, event | category | flops | bytes accessed | tf_op | source)
XLA Modules:
  0.0 206.2 jit_solution(17440413600158368)
XLA Ops:
  5.3 3.0 %collective-permute-start = (bf16[1,2,160,768]{3,2,1,0:T(8,128)(2,1)S(1)}, bf16[1,2,160,768]{3,2,1,0:T(8,128)(2,1)S(1)}, u32[]{:S(2)}, u32[]{:S(2)}) collective-permute-start(bf16[1,2,160,768]{3,2,1,0:T(8,128)(2,1)S(1)} %get-tuple-element.14), channel_id=1, source_target_pairs={{0,4},{4,8},{8,12},{12,0},{1,5},{5,9},{9,13},{13,1},{2,6},{6,10},{... | collective-permute-start | bytes 1474568 | tf_op jit(solution)/shard_map/ppermute | solution.py:16
  8.3 2.1 collective-permute-start.1
  10.4 12.1 %collective-permute-done = bf16[1,2,160,768]{3,2,1,0:T(8,128)(2,1)S(1)} collective-permute-done((bf16[1,2,160,768]{3,2,1,0:T(8,128)(2,1)S(1)}, bf16[1,2,160,768]{3,2,1,0:T(8,128)(2,1)S(1)}, u32[]{:S(2)}, u32[]{:S(2)}) %collective-permute-start) | collective-permute-done | bytes 491552 | tf_op jit(solution)/shard_map/ppermute | solution.py:16
  23.3 8.4 %collective-permute-done.1 = bf16[1,2,160,768]{3,2,1,0:T(8,128)(2,1)S(1)} collective-permute-done((bf16[1,2,160,768]{3,2,1,0:T(8,128)(2,1)S(1)}, bf16[1,2,160,768]{3,2,1,0:T(8,128)(2,1)S(1)}, u32[]{:S(2)}, u32[]{:S(2)}) %collective-permute-start.1) | collective-permute-done | bytes 491552 | tf_op jit(solution)/shard_map/ppermute | solution.py:19
  32.5 10.2 %collective-permute-done.2 = bf16[1,2,160,768]{3,2,1,0:T(8,128)(2,1)S(1)} collective-permute-done((bf16[1,2,160,768]{3,2,1,0:T(8,128)(2,1)S(1)}, bf16[1,2,160,768]{3,2,1,0:T(8,128)(2,1)S(1)}, u32[]{:S(2)}, u32[]{:S(2)}) %collective-permute-start.2) | collective-permute-done | bytes 491552 | tf_op jit(solution)/shard_map/ppermute | solution.py:16
  43.5 1.7 fusion.61
  45.2 1.6 collective-permute-start.3
  49.1 3.8 %collective-permute-start.5 = (bf16[3,1,160,384]{3,2,1,0:T(8,128)(2,1)}, bf16[3,1,160,384]{3,2,1,0:T(8,128)(2,1)}, u32[]{:S(2)}, u32[]{:S(2)}) collective-permute-start(bf16[3,1,160,384]{3,2,1,0:T(8,128)(2,1)} %get-tuple-element.12), channel_id=1, source_target_pairs={{0,1},{1,2},{2,3},{4,5},{5,6},{6,7},{8,9},{9,10},{10,11},{12,13},{... | collective-permute-start | bytes 1105928 | tf_op jit(solution)/shard_map/ppermute | solution.py:40
  52.9 16.1 %collective-permute-done.3 = bf16[4,2,160,384]{3,2,1,0:T(8,128)(2,1)S(1)} collective-permute-done((bf16[4,2,160,384]{3,2,1,0:T(8,128)(2,1)S(1)}, bf16[4,2,160,384]{3,2,1,0:T(8,128)(2,1)S(1)}, u32[]{:S(2)}, u32[]{:S(2)}) %collective-permute-start.3) | collective-permute-done | bytes 983072 | tf_op jit(solution)/shard_map/ppermute | solution.py:133
  69.0 1.6 pad_maximum_fusion.1
  70.6 3.0 %copy.52 = bf16[4,2,160,384]{2,1,0,3:T(2,128)(2,1)} copy(bf16[4,2,160,384]{3,2,1,0:T(8,128)(2,1)S(1)} %get-tuple-element.8) | data formatting | bytes 1966080 | tf_op jit(solution)/shard_map/slice | solution.py:183
  73.7 3.9 %all-to-all-start = ((bf16[4,2,160,384]{2,1,0,3:T(2,128)(2,1)}), bf16[4,2,160,384]{2,1,0,3:T(2,128)(2,1)S(1)}, u32[]{:S(2)}, u32[]{:S(2)}) async-start(bf16[4,2,160,384]{2,1,0,3:T(2,128)(2,1)} %copy.52), calls=%async_computation | async-start | bytes 3145728 | tf_op jit(solution)/shard_map/all_to_all | solution.py:184
  77.7 1.6 fusion.40
  81.1 7.0 %fusion.41 = f32[1,2,8,21,384]{4,2,3,1,0:T(8,128)S(1)} fusion(bf16[3,3,3,384,384]{4,3,2,1,0:T(8,128)(2,1)} %bitcast.51, bf16[3,4,1,7,2,384]{5,3,4,1,0,2:T(8,128)(2,1)S(1)} %slice.34, bf16[3,4,1,8,21,384]{5,3,4,1,0,2:T(8,128)(2,1)S(1)} %copy.49, pred[8,21]{0,1:T(8,128)(4,1)S(1)} %copy-done.11), kind=kOutput, calls=%fused_computation.59 | convolution fusion | flops 2680657920 | bytes 10156200 | tf_op jit(solution)/shard_map/conv_general_dilated | solution.py:74
  89.9 8.4 %all-to-all-done = bf16[4,2,160,384]{2,1,0,3:T(2,128)(2,1)S(1)} async-done(((bf16[4,2,160,384]{2,1,0,3:T(2,128)(2,1)}), bf16[4,2,160,384]{2,1,0,3:T(2,128)(2,1)S(1)}, u32[]{:S(2)}, u32[]{:S(2)}) %all-to-all-start) | async-done | bytes 983072 | tf_op jit(solution)/shard_map/all_to_all | solution.py:184
  98.3 4.4 %copy.58 = bf16[4,2,160,4,96]{4,3,2,1,0:T(4,128)(2,1)} copy(bf16[4,2,160,4,96]{2,1,0,4,3:T(2,128)(2,1)S(1)} %bitcast.44) | data formatting | bytes 1966080 | tf_op jit(solution)/shard_map/all_to_all | solution.py:184
  104.2 1.7 fusion.62
  107.5 1.6 fusion.20
  109.2 5.9 %fusion.10 = bf16[6,10,162,384]{3,2,1,0:T(8,128)(2,1)S(1)} fusion(bf16[4,4,160,384]{3,2,1,0:T(8,128)(2,1)S(1)} %get-tuple-element.7, bf16[4,4,160,384]{3,2,1,0:T(8,128)(2,1)S(1)} %get-tuple-element.6), kind=kLoop, calls=%fused_computation.15 | loop fusion | flops 70917120 | bytes 11397120 | tf_op jit(solution)/shard_map/concatenate | solution.py:153
  117.1 3.9 %fusion.44 = f32[1,2,8,21,384]{4,2,3,1,0:T(8,128)S(1)} fusion(bf16[3,3,3,384,384]{4,3,2,1,0:T(8,128)(2,1)S(1)} %bitcast.54, bf16[3,4,1,7,2,384]{5,3,4,1,0,2:T(8,128)(2,1)S(1)} %slice.31, bf16[3,4,1,8,21,384]{5,3,4,1,0,2:T(8,128)(2,1)S(1)} %copy.44, pred[8,21]{0,1:T(8,128)(4,1)S(1)} %copy-done.11), kind=kOutput, calls=%fused_computation.60 | convolution fusion | flops 2680657920 | bytes 10156200 | tf_op jit(solution)/shard_map/conv_general_dilated | solution.py:61
  122.8 74.8 %fusion.6 = f32[2,3,3,384,96]{3,4,2,1,0:T(8,128)S(1)} fusion(bf16[5,10,162,384,1]{3,2,1,0,4:T(8,128)(2,1)S(1)} %dynamic-slice_bitcast_fusion, bf16[4,8,160,1,96]{4,2,1,0,3:T(8,128)(2,1)S(1)} %bitcast.50), kind=kOutput, calls=%fused_computation.11 | convolution fusion | flops 6794772480 | bytes 9858048 | tf_op jit(solution)/shard_map/conv_general_dilated | solution.py:113
  197.6 1.8 copy.57
  199.4 2.8 %reshape.42 = f32[6912,96]{0,1:T(8,128)} reshape(f32[2,3,3,384,96]{3,2,1,0,4:T(4,128)S(1)} %copy.57) | data formatting | bytes 5308416 | tf_op jit(solution)/shard_map/reshape | solution.py:120
  202.3 2.6 %dynamic-slice_multiply_fusion = f32[2592,96]{0,1:T(8,128)} fusion(f32[6912,96]{0,1:T(8,128)} %reshape.42, s32[]{:T(128)S(6)} %select_n.97), kind=kLoop, calls=%fused_computation.61 | loop fusion | flops 248832 | bytes 1990660 | tf_op jit(solution)/shard_map/mul | solution.py:195
  (65 shorter events, 21.2 us)
Async XLA Ops:
  0.6 3.8 %copy-start.7 = (bf16[1,2,160,384]{3,2,1,0:T(8,128)(2,1)S(1)}, bf16[1,2,160,384]{3,2,1,0:T(8,128)(2,1)}, u32[]{:S(2)}) copy-start(bf16[1,2,160,384]{3,2,1,0:T(8,128)(2,1)} %param.9) | copy-start | bytes 737284
  5.3 17.2 %collective-permute-start = (bf16[1,2,160,768]{3,2,1,0:T(8,128)(2,1)S(1)}, bf16[1,2,160,768]{3,2,1,0:T(8,128)(2,1)S(1)}, u32[]{:S(2)}, u32[]{:S(2)}) collective-permute-start(bf16[1,2,160,768]{3,2,1,0:T(8,128)(2,1)S(1)} %get-tuple-element.14), channel_id=1, source_target_pairs={{0,4},{4,8},{8,12},{12,0},{1,5},{5,9},{9,13},{13,1},{2,6},{6,10},{... | collective-permute-start | bytes 1474568 | tf_op jit(solution)/shard_map/ppermute | solution.py:16
  8.3 23.4 %collective-permute-start.1 = (bf16[1,2,160,768]{3,2,1,0:T(8,128)(2,1)S(1)}, bf16[1,2,160,768]{3,2,1,0:T(8,128)(2,1)S(1)}, u32[]{:S(2)}, u32[]{:S(2)}) collective-permute-start(bf16[1,2,160,768]{3,2,1,0:T(8,128)(2,1)S(1)} %get-tuple-element.14), channel_id=1, source_target_pairs={{0,12},{4,0},{8,4},{12,8},{1,13},{5,1},{9,5},{13,9},{2,14},{6,2},{... | collective-permute-start | bytes 1474568 | tf_op jit(solution)/shard_map/ppermute | solution.py:19
  22.5 20.2 %collective-permute-start.2 = (bf16[1,2,160,768]{3,2,1,0:T(8,128)(2,1)S(1)}, bf16[1,2,160,768]{3,2,1,0:T(8,128)(2,1)S(1)}, u32[]{:S(2)}, u32[]{:S(2)}) collective-permute-start(bf16[1,2,160,768]{3,2,1,0:T(8,128)(2,1)S(1)} %collective-permute-done), channel_id=1, source_target_pairs={{0,4},{4,8},{8,12},{12,0},{1,5},{5,9},{9,13},{13,1},{2,6},{6,10},{... | collective-permute-start | bytes 1474568 | tf_op jit(solution)/shard_map/ppermute | solution.py:16
  45.2 23.8 %collective-permute-start.3 = (bf16[4,2,160,384]{3,2,1,0:T(8,128)(2,1)S(1)}, bf16[4,2,160,384]{3,2,1,0:T(8,128)(2,1)S(1)}, u32[]{:S(2)}, u32[]{:S(2)}) collective-permute-start(bf16[4,2,160,384]{3,2,1,0:T(8,128)(2,1)S(1)} %get-tuple-element.9), channel_id=1, source_target_pairs={{0,2},{1,3},{2,0},{3,1},{4,6},{5,7},{6,4},{7,5},{8,10},{9,11},{10,... | collective-permute-start | bytes 2949128 | tf_op jit(solution)/shard_map/ppermute | solution.py:133
  47.8 29.9 %collective-permute-start.6 = (bf16[3,1,160,384]{3,2,1,0:T(8,128)(2,1)}, bf16[3,1,160,384]{3,2,1,0:T(8,128)(2,1)}, u32[]{:S(2)}, u32[]{:S(2)}) collective-permute-start(bf16[3,1,160,384]{3,2,1,0:T(8,128)(2,1)} %get-tuple-element.13), channel_id=1, source_target_pairs={{1,0},{2,1},{3,2},{5,4},{6,5},{7,6},{9,8},{10,9},{11,10},{13,12},{... | collective-permute-start | bytes 1105928 | tf_op jit(solution)/shard_map/ppermute | solution.py:42
  49.1 28.6 %collective-permute-start.5 = (bf16[3,1,160,384]{3,2,1,0:T(8,128)(2,1)}, bf16[3,1,160,384]{3,2,1,0:T(8,128)(2,1)}, u32[]{:S(2)}, u32[]{:S(2)}) collective-permute-start(bf16[3,1,160,384]{3,2,1,0:T(8,128)(2,1)} %get-tuple-element.12), channel_id=1, source_target_pairs={{0,1},{1,2},{2,3},{4,5},{5,6},{6,7},{8,9},{9,10},{10,11},{12,13},{... | collective-permute-start | bytes 1105928 | tf_op jit(solution)/shard_map/ppermute | solution.py:40
  69.0 1.6 copy-start.4
  70.6 33.6 %collective-permute-start.4 = (bf16[4,4,160,384]{3,2,1,0:T(8,128)(2,1)}, bf16[4,4,160,384]{3,2,1,0:T(8,128)(2,1)}, u32[]{:S(2)}, u32[]{:S(2)}) collective-permute-start(bf16[4,4,160,384]{3,2,1,0:T(8,128)(2,1)} %pad_maximum_fusion.1), channel_id=1, source_target_pairs={{0,1},{1,0},{2,3},{3,2},{4,5},{5,4},{6,7},{7,6},{8,9},{9,8},{10,11... | collective-permute-start | bytes 5898248 | tf_op jit(solution)/shard_map/ppermute | solution.py:139
  73.7 24.6 %all-to-all-start = ((bf16[4,2,160,384]{2,1,0,3:T(2,128)(2,1)}), bf16[4,2,160,384]{2,1,0,3:T(2,128)(2,1)S(1)}, u32[]{:S(2)}, u32[]{:S(2)}) async-start(bf16[4,2,160,384]{2,1,0,3:T(2,128)(2,1)} %copy.52), calls=%async_computation | async-start | bytes 3145728 | tf_op jit(solution)/shard_map/all_to_all | solution.py:184
  80.4 0.7 copy-start.11
  88.1 0.9 copy-start.2
  88.1 0.9 copy-start.9
  89.1 0.8 copy-start
  106.0 1.2 copy-start.5
  109.1 7.5 %slice-start = ((s8[7962624]{0:T(1024)(128)(4,1)}), s8[4194304]{0:T(1024)(128)(4,1)S(1)}, s32[]{:S(2)}) async-start(s8[7962624]{0:T(1024)(128)(4,1)} %bitcast.52), calls=%async_computation.1 | async-start | bytes 8388608
  115.0 2.1 %slice-start.1 = ((s8[7962624]{0:T(1024)(128)(4,1)}), s8[3768320]{0:T(1024)(128)(4,1)S(1)}, s32[]{:S(2)}) async-start(s8[7962624]{0:T(1024)(128)(4,1)} %bitcast.52), calls=%async_computation.2 | async-start | bytes 7536640
  202.3 2.7 %copy-start.1 = (f32[1,2,1,160,384]{4,1,3,2,0:T(2,128)S(1)}, f32[1,2,1,160,384]{4,1,3,2,0:T(2,128)}, u32[]{:S(2)}) copy-start(f32[1,2,1,160,384]{4,1,3,2,0:T(2,128)} %copy-done) | copy-start | bytes 1474564
  202.3 2.7 %copy-start.3 = (bf16[1,2,160,384]{3,2,1,0:T(8,128)(2,1)S(1)}, bf16[1,2,160,384]{3,2,1,0:T(8,128)(2,1)}, u32[]{:S(2)}) copy-start(bf16[1,2,160,384]{3,2,1,0:T(8,128)(2,1)} %param.5) | copy-start | bytes 737284
  202.3 2.7 %copy-start.6 = (f32[1,2,1,160,384]{4,1,3,2,0:T(2,128)S(1)}, f32[1,2,1,160,384]{4,1,3,2,0:T(2,128)}, u32[]{:S(2)}) copy-start(f32[1,2,1,160,384]{4,1,3,2,0:T(2,128)} %slice.32) | copy-start | bytes 1474564
  202.3 2.7 %copy-start.8 = (bf16[1,2,160,384]{3,2,1,0:T(8,128)(2,1)S(1)}, bf16[1,2,160,384]{3,2,1,0:T(8,128)(2,1)}, u32[]{:S(2)}) copy-start(bf16[1,2,160,384]{3,2,1,0:T(8,128)(2,1)} %param.9) | copy-start | bytes 737284
  202.3 2.7 %copy-start.10 = (f32[384]{0:T(512)S(1)}, f32[384]{0:T(512)}, u32[]{:S(2)}) copy-start(f32[384]{0:T(512)} %param.7) | copy-start | bytes 4612
